TPU v7x, 256 devices: a whole 4x4x8 slice. The times are simulated.
256 devices in a mesh: req: 32 (over x, y, core), tp: 8 (over z).
Axes of the slice: x: 4, y: 4, z: 8, core: 2. Of those that a mesh axis runs over, the one named last changes fastest.
Arguments:
- query: bfloat16 [768, 4096], P('req', 'tp'), may hold values from -102 to 102
- new_key: bfloat16 [768, 1024], P('req', 'tp'), may hold values from -6 to 6
- new_value: bfloat16 [768, 1024], P('req', 'tp'), may hold values from -6 to 6
- prefix_key: bfloat16 [64, 6144, 1024], P('req', None, 'tp'), may hold values from -6 to 6
- prefix_value: bfloat16 [64, 6144, 1024], P('req', None, 'tp'), may hold values from -6 to 6
- suffix_key: bfloat16 [768, 128, 1024], P('req', None, 'tp'), may hold values from -6 to 6
- suffix_value: bfloat16 [768, 128, 1024], P('req', None, 'tp'), may hold values from -6 to 6
- group_ids: int32 [768], replicated, may hold values from 0 to 63, as said below
- prompt_len: int32 [64], P('req'), may hold values from 768 to 6144, as said below
- suffix_len: int32 [768], replicated, may hold values from 1 to 128, as said below
- o_weight: bfloat16 [4096, 4096], P('tp'), may hold values from -0.09375 to 0.09375
- residual: bfloat16 [768, 4096], P('req'), may hold values from -0.29882812 to 0.29882812
- norm_gain: bfloat16 [4096], replicated, may hold values from 0.5 to 1.5
Outputs:
- hidden: bfloat16 [768, 4096], P('req')
- normed: bfloat16 [768, 4096], P('req')
Inputs may be any that keep to these rules, and one draw needn't show every extreme that they name: Request r belongs to group group_ids[r]; groups 2k to 2k + 1 at a time are held together (group // 2 names the holder). Among each aligned block of 24 requests, every holder that appears is named by exactly 2 of them. `prompt_len`: some group has exactly 6144. `suffix_len`: some request has exactly 128.
All inputs are finite; a program needn't handle non-finite values.
Results may differ from a plain program's by a relative error of at most 0.008.
Values may be sent and summed in bfloat16 or wider, within the bound.
No kernel may reach another device: no remote copies, remote signals or barrier semaphores. Data moves between devices by JAX's collectives and lax.ppermute only.
A program may use at most 64 MiB of HBM per device.

v0:
```python
import math
import jax
import jax.numpy as jnp
from jax import lax
from jax.sharding import PartitionSpec as P

HD = 128
WIN = 4096
SINKS = 4
FAR_BELOW = -1e30
NORM_EPS = 1e-06


def prefix_attend(
    rows_query, row_group, row_suffix, prefix_key, prefix_value, prompt_len, first_group, blocks
):
    row_count = rows_query.shape[0]
    groups_dev = prefix_key.shape[0]
    prompt_max = prefix_key.shape[1]
    kv_dev = prefix_key.shape[2] // HD
    heads_dev = rows_query.shape[1] // HD
    repeat = heads_dev // kv_dev
    block_len = min(512, prompt_max)
    score_scale = 1.0 / math.sqrt(HD)
    local_group = row_group - first_group
    owned = (local_group >= 0) & (local_group < groups_dev)
    member = local_group[:, None] == jnp.arange(groups_dev, dtype=jnp.int32)[None, :]
    row_prompt = jnp.sum(jnp.where(member, prompt_len[None, :], 0), axis=1)
    row_low = row_prompt + row_suffix - WIN + 1
    queries = rows_query.reshape(row_count, kv_dev, repeat, HD)

    def key_step(block_index, loop_state):
        running, weight_sum, weighted = loop_state
        key_start = block_index * block_len
        key_block = lax.dynamic_slice_in_dim(prefix_key, key_start, block_len, 1).reshape(
            groups_dev, block_len, kv_dev, HD
        )
        value_block = lax.dynamic_slice_in_dim(prefix_value, key_start, block_len, 1).reshape(
            groups_dev, block_len, kv_dev, HD
        )
        scores = (
            jnp.einsum("rkhd,gpkd->rkhgp", queries, key_block, preferred_element_type=jnp.float32)
            * score_scale
        )
        positions = key_start + jnp.arange(block_len, dtype=jnp.int32)
        inside = positions[None, :] < prompt_len[:, None]
        window = (positions[None, :] < SINKS) | (positions[None, :] >= row_low[:, None])
        usable = member[:, :, None] & inside[None, :, :] & window[:, None, :]
        usable = usable[:, None, None, :, :]
        masked = jnp.where(usable, scores, FAR_BELOW)
        updated = jnp.maximum(running, jnp.max(masked, axis=(3, 4)))
        weights = jnp.where(usable, jnp.exp(masked - updated[..., None, None]), 0.0)
        rescale = jnp.exp(running - updated)
        weight_sum = weight_sum * rescale + jnp.sum(weights, axis=(3, 4))
        rounded = weights.astype(jnp.bfloat16)
        weighted = weighted * rescale[..., None] + jnp.einsum(
            "rkhgp,gpkd->rkhd", rounded, value_block, preferred_element_type=jnp.float32
        )
        return (updated, weight_sum, weighted)

    initial = (
        jnp.full((row_count, kv_dev, repeat), FAR_BELOW, jnp.float32),
        jnp.zeros((row_count, kv_dev, repeat), jnp.float32),
        jnp.zeros((row_count, kv_dev, repeat, HD), jnp.float32),
    )
    running, weight_sum, weighted = lax.fori_loop(0, blocks, key_step, initial)
    bounded = jnp.maximum(weight_sum, 1.0)
    normalized = jnp.where(owned[:, None, None, None], weighted / bounded[..., None], 0.0).reshape(
        row_count, heads_dev * HD
    )
    log_total = jnp.where(owned[:, None, None], running + jnp.log(bounded), 0.0).reshape(
        row_count, heads_dev
    )
    return (normalized, log_total)


def body(
    query,
    new_key,
    new_value,
    prefix_key,
    prefix_value,
    suffix_key,
    suffix_value,
    group_ids,
    prompt_len,
    suffix_len,
    o_weight,
    residual,
    norm_gain,
):
    req_dev = query.shape[0]
    heads_dev = query.shape[1] // HD
    kv_dev = new_key.shape[1] // HD
    repeat = heads_dev // kv_dev
    groups_dev = prefix_key.shape[0]
    prompt_max = prefix_key.shape[1]
    suffix_max = suffix_key.shape[1]
    block_len = min(512, prompt_max)
    score_scale = 1.0 / math.sqrt(HD)
    places = lax.axis_size("req")
    device = lax.axis_index("req")
    first_group = device * groups_dev
    own_suffix = lax.dynamic_slice_in_dim(suffix_len, device * req_dev, req_dev)
    blocks = prompt_max // block_len
    capacity = max(2, req_dev // places)
    slot_total = places * capacity
    all_groups = group_ids.reshape(places, 1, req_dev)
    all_suffix = suffix_len.reshape(places, 1, req_dev)
    all_rows = (
        jnp.arange(places, dtype=jnp.int32)[:, None] * req_dev
        + jnp.arange(req_dev, dtype=jnp.int32)[None, :]
    ).reshape(places, 1, req_dev)
    is_mine = (group_ids // groups_dev).reshape(places, req_dev) == device
    slot_order = jnp.cumsum(is_mine.astype(jnp.int32), axis=1) - 1
    slot_pick = is_mine[:, None, :] & (
        slot_order[:, None, :] == jnp.arange(capacity, dtype=jnp.int32)[None, :, None]
    )
    filled = jnp.any(slot_pick, axis=2)
    slot_group = jnp.where(
        filled, jnp.sum(jnp.where(slot_pick, all_groups, 0), axis=2), -1
    ).reshape(slot_total)
    slot_suffix = jnp.sum(jnp.where(slot_pick, all_suffix, 0), axis=2).reshape(slot_total)
    slot_row = jnp.where(filled, jnp.sum(jnp.where(slot_pick, all_rows, 0), axis=2), -1).reshape(
        slot_total
    )
    every_query = lax.all_gather(query, "req", axis=0, tiled=True)
    pick_rows = slot_row[:, None] == jnp.arange(places * req_dev, dtype=jnp.int32)[None, :]
    compact = jnp.dot(
        pick_rows.astype(jnp.bfloat16), every_query, preferred_element_type=jnp.float32
    ).astype(jnp.bfloat16)
    part_out, part_log = prefix_attend(
        compact, slot_group, slot_suffix, prefix_key, prefix_value, prompt_len, first_group, blocks
    )
    spread_rows = pick_rows.T.astype(jnp.float32)
    spread_out = jnp.dot(spread_rows, part_out, precision=lax.Precision.HIGHEST)
    spread_log = jnp.dot(spread_rows, part_log, precision=lax.Precision.HIGHEST)
    prefix_out, prefix_log = (
        lax.psum_scatter(spread_out, "req", scatter_dimension=0, tiled=True),
        lax.psum_scatter(spread_log, "req", scatter_dimension=0, tiled=True),
    )
    queries = query.reshape(req_dev, kv_dev, repeat, HD)
    key_rows = suffix_key.reshape(req_dev, suffix_max, kv_dev, HD)
    value_rows = suffix_value.reshape(req_dev, suffix_max, kv_dev, HD)
    scores = (
        jnp.einsum("rkhd,rjkd->rkhj", queries, key_rows, preferred_element_type=jnp.float32)
        * score_scale
    )
    own_score = (
        jnp.einsum(
            "rkhd,rkd->rkh",
            queries,
            new_key.reshape(req_dev, kv_dev, HD),
            preferred_element_type=jnp.float32,
        )
        * score_scale
    )
    usable = (jnp.arange(suffix_max, dtype=jnp.int32)[None, :] < own_suffix[:, None])[
        :, None, None, :
    ]
    masked = jnp.where(usable, scores, FAR_BELOW)
    running = jnp.maximum(jnp.max(masked, axis=-1), own_score)
    weights = jnp.where(usable, jnp.exp(masked - running[..., None]), 0.0)
    own_weight = jnp.exp(own_score - running)
    weight_sum = jnp.sum(weights, axis=-1) + own_weight
    weighted = jnp.einsum(
        "rkhj,rjkd->rkhd",
        weights.astype(jnp.bfloat16),
        value_rows,
        preferred_element_type=jnp.float32,
    )
    own_rounded = own_weight.astype(jnp.bfloat16).astype(jnp.float32)
    weighted = weighted + own_rounded[..., None] * new_value.reshape(req_dev, kv_dev, 1, HD).astype(
        jnp.float32
    )
    local_out = weighted / weight_sum[..., None]
    local_log = running + jnp.log(weight_sum)
    prefix_out = prefix_out.reshape(req_dev, kv_dev, repeat, HD)
    prefix_log = prefix_log.reshape(req_dev, kv_dev, repeat)
    combined = jnp.logaddexp(prefix_log, local_log)
    attended = (
        prefix_out * jnp.exp(prefix_log - combined)[..., None]
        + local_out * jnp.exp(local_log - combined)[..., None]
    )
    attended = attended.reshape(req_dev, heads_dev * HD).astype(jnp.bfloat16)
    partial_value = jnp.dot(attended, o_weight, preferred_element_type=jnp.float32)
    proj = lax.psum(partial_value, "tp")
    summed = residual.astype(jnp.float32) + proj
    hidden = summed.astype(jnp.bfloat16)
    inverse = lax.rsqrt(jnp.mean(summed * summed, axis=-1, keepdims=True) + NORM_EPS)
    normed = (summed * inverse * norm_gain.astype(jnp.float32)[None, :]).astype(jnp.bfloat16)
    return (hidden, normed)


def solution(mesh):
    placed = (
        P("req", "tp"),
        P("req", "tp"),
        P("req", "tp"),
        P("req", None, "tp"),
        P("req", None, "tp"),
        P("req", None, "tp"),
        P("req", None, "tp"),
        P(),
        P("req"),
        P(),
        P("tp", None),
        P("req", None),
        P(),
    )
    return jax.shard_map(
        body,
        mesh=mesh,
        in_specs=placed,
        out_specs=(P("req", None), P("req", None)),
        check_vma=False,
    )
```

profile of v0, /device:TPU:2, one launch (start us, length us, event | category | flops | bytes accessed | tf_op | source)
XLA Modules:
  0.0 305.6 jit_solution(10688126659396240701)
XLA Ops:
  11.4 24.9 %all_gather.3 = bf16[768,512]{1,0:T(8,128)(2,1)S(1)} all-gather(bf16[24,512]{1,0:T(8,128)(2,1)} %param.15), channel_id=1, replica_groups=mesh['req'=32,'tp'=8] {'req'}, dimensions={0}, use_global_device_ids=true | all-gather | bytes 811008 | tf_op jit(solution)/shard_map/all_gather | solution.py:127
  36.8 50.0 %while.18 = (s32[]{:T(128)}, f32[64,1,4]{0,2,1:T(4,128)S(1)}, f32[64,1,4]{0,2,1:T(4,128)S(1)}, f32[64,1,4,128]{3,0,2,1:T(8,128)S(1)}, s32[2]{0:T(128)}, /*index=...) while((s32[]{:T(128)}, f32[64,1,4]{0,2,1:T(4,128)S(1)}, ...), condition=%wide.region_9.10_spmd.clone, body=%wide.region_6.9_spmd.clone.sunk | while | flops 136876160 | bytes 4351967 | solution.py:66
  37.8 1.4 fusion.83
  39.6 1.4 fusion.86
  42.0 1.4 fusion.83
  43.8 1.4 fusion.86
  47.9 1.4 fusion.86
  52.1 1.4 fusion.86
  56.3 1.4 fusion.86
  58.7 1.4 fusion.83
  60.5 1.4 fusion.86
  62.9 1.4 fusion.83
  64.6 1.4 fusion.86
  68.8 1.4 fusion.86
  73.0 1.4 fusion.86
  77.1 1.4 fusion.86
  81.3 1.4 fusion.86
  83.7 1.4 fusion.83
  85.5 1.4 fusion.86
  87.2 2.0 fusion.27
  91.6 109.0 %all-reduce = f32[768,4]{0,1:T(4,128)S(1)} all-reduce(f32[768,4]{0,1:T(4,128)S(1)} %fusion.26), channel_id=3, replica_groups=mesh['req'=32,'tp'=8] {'req'}, use_global_device_ids=true, to_apply=%region_11.12.clone | all-reduce | flops 3072 | bytes 24576
  203.2 3.6 %fusion.37 = f32[24,4096]{1,0:T(8,128)} fusion(bf16[512,4096]{1,0:T(8,128)(2,1)} %param.25, bf16[3,8,4,128]{3,2,1,0:T(4,128)(2,1)S(1)} %bitcast.93), kind=kOutput, calls=%fused_computation.57 | convolution fusion | flops 100663296 | bytes 4612096 | tf_op jit(solution)/shard_map/dot_general | solution.py:186
  206.8 88.9 %all-reduce.3.cloned.1.call-done = f32[24,4096]{1,0:T(8,128)} async-done(((f32[24,4096]{1,0:T(8,128)}), f32[24,4096]{1,0:T(8,128)}) %all-reduce.3.cloned.1.call-update) | async-done | bytes 393232 | tf_op jit(solution)/shard_map/psum | solution.py:187
  297.0 1.8 multiply_convert_fusion
  (201 shorter events, 35.8 us)
Async XLA Ops:
  7.2 193.8 %copy-start = (bf16[24,128,128]{2,1,0:T(8,128)(2,1)S(1)}, bf16[24,128,128]{2,1,0:T(8,128)(2,1)}, u32[]{:S(2)}) copy-start(bf16[24,128,128]{2,1,0:T(8,128)(2,1)} %param.20) | copy-start | bytes 2359300
  7.2 194.8 %reduce-scatter.3.cloned.1.call-start = ((), (), s32[]{:S(2)}) async-start(), calls=%async_computation.1 | async-start | bytes 1622016 | tf_op jit(solution)/shard_map/reduce_scatter | solution.py:139
  86.9 2.4 copy-start.2
  86.9 3.2 %copy-start.7 = (u32[256]{0:T(256)S(1)}, u32[256]{0:T(256)}, u32[]{:S(2)}) copy-start(u32[256]{0:T(256)} %constant.130) | copy-start | bytes 3076
  86.9 113.9 %copy-start.4 = (bf16[24,128]{1,0:T(8,128)(2,1)S(1)}, bf16[24,128]{1,0:T(8,128)(2,1)}, u32[]{:S(2)}) copy-start(bf16[24,128]{1,0:T(8,128)(2,1)} %param.17) | copy-start | bytes 18436
  86.9 113.9 %copy-start.6 = (bf16[24,128]{1,0:T(8,128)(2,1)S(1)}, bf16[24,128]{1,0:T(8,128)(2,1)}, u32[]{:S(2)}) copy-start(bf16[24,128]{1,0:T(8,128)(2,1)} %param.16) | copy-start | bytes 18436
  86.9 115.8 %copy-start.5 = (bf16[24,128,128]{2,1,0:T(8,128)(2,1)S(1)}, bf16[24,128,128]{2,1,0:T(8,128)(2,1)}, u32[]{:S(2)}) copy-start(bf16[24,128,128]{2,1,0:T(8,128)(2,1)} %param.21) | copy-start | bytes 2359300
  89.2 206.5 %all-reduce.3.cloned.1.call-start = ((), (), s32[]{:S(2)}) async-start(), calls=%async_computation.2 | async-start | bytes 786432 | tf_op jit(solution)/shard_map/psum | solution.py:187
  202.8 4.0 %copy-start.3 = (bf16[4096]{0:T(1024)(128)(2,1)S(1)}, bf16[4096]{0:T(1024)(128)(2,1)}, u32[]{:S(2)}) copy-start(bf16[4096]{0:T(1024)(128)(2,1)} %param.27) | copy-start | bytes 24580
  202.8 93.0 %copy-start.1 = (bf16[24,4096]{1,0:T(8,128)(2,1)S(1)}, bf16[24,4096]{1,0:T(8,128)(2,1)}, u32[]{:S(2)}) copy-start(bf16[24,4096]{1,0:T(8,128)(2,1)} %param.26) | copy-start | bytes 589828
Sparse Core Ops, SparseCore 0:
  89.4 86.8 reduce-scatter.2
  206.9 88.8 all-reduce.2
where the time goes:
time: 307 us; the launch traced here: 306 us
  blocking collectives  134 us (44%)
  waiting for transfers between devices  89 us (29%)
  matrix products  40.4 us (13%)
  other arithmetic  21.3 us (7%)
  between operations  15 us (5%)
  local copies, waits for them, and re-layouts  5.04 us (2%)
    unnamed x1, blocking collectives  109 us
    psum x1, waiting for transfers between devices, body(): proj = lax.psum(partial_value, 'tp')  88.9 us
    all_gather x1, blocking collectives, body(): every_query = lax.all_gather(query, 'req', axis=0, tiled=True)  24.9 us
    dot_general x12, matrix products, key_step(): jnp.einsum('rkhgp,gpkd->rkhd', rounded, value_block, preferred_element_ty...  16.8 us
    dot_general x12, matrix products, key_step(): jnp.einsum('rkhd,gpkd->rkhgp', queries, key_block, preferred_element_type...  16.3 us
    lt x12, other arithmetic, key_step(): inside = positions[None, :] < prompt_len[:, None]  8.77 us
  transfers between devices with their start and end apart: 2, of which 1 were waited for; matrix products, arithmetic and copies ran while one was open for 1% of the time, Pallas kernels for 0%

commit v1 on v0

--- a/solution.py
+++ b/solution.py
@@ -9,6 +9,14 @@
 SINKS = 4
 FAR_BELOW = -1e30
 NORM_EPS = 1e-06
+
+
+def doubling_sum(x, axis):
+    size, summed = (lax.axis_size(axis), x)
+    for far in [1 << k for k in range(size.bit_length() - 1)]:
+        swap = [(i, i ^ far) for i in range(size)]
+        summed = summed + lax.ppermute(summed, axis, swap)
+    return summed
 
 
 def prefix_attend(
@@ -184,7 +192,7 @@
     )
     attended = attended.reshape(req_dev, heads_dev * HD).astype(jnp.bfloat16)
     partial_value = jnp.dot(attended, o_weight, preferred_element_type=jnp.float32)
-    proj = lax.psum(partial_value, "tp")
+    proj = doubling_sum(partial_value, "tp")
     summed = residual.astype(jnp.float32) + proj
     hidden = summed.astype(jnp.bfloat16)
     inverse = lax.rsqrt(jnp.mean(summed * summed, axis=-1, keepdims=True) + NORM_EPS)

time: 307 us -> 280 us (0.912)
  the two profiles are of different devices: /device:TPU:2 before, /device:TPU:30 now
where the time goes in v1:
time: 280 us; the launch traced here: 278 us
  blocking collectives  143 us (51%)
  waiting for transfers between devices  42.4 us (15%)
  matrix products  39.6 us (14%)
  other arithmetic  19.3 us (7%)
  between operations  15 us (5%)
  starting transfers between devices  13.2 us (5%)
  local copies, waits for them, and re-layouts  5.03 us (2%)
    unnamed x1, blocking collectives  120 us
    ppermute x3, waiting for transfers between devices, doubling_sum(): summed = summed + lax.ppermute(summed, axis, swap)  42.4 us
    all_gather x1, blocking collectives, body(): every_query = lax.all_gather(query, 'req', axis=0, tiled=True)  22.6 us
    dot_general x12, matrix products, key_step(): jnp.einsum('rkhgp,gpkd->rkhd', rounded, value_block, preferred_element_ty...  16.8 us
    dot_general x12, matrix products, key_step(): jnp.einsum('rkhd,gpkd->rkhgp', queries, key_block, preferred_element_type...  16.2 us
    ppermute x3, starting transfers between devices, doubling_sum(): summed = summed + lax.ppermute(summed, axis, swap)  13.1 us
    lt x12, other arithmetic, key_step(): inside = positions[None, :] < prompt_len[:, None]  8.77 us
  transfers between devices with their start and end apart: 4, of which 3 were waited for; matrix products, arithmetic and copies ran while one was open for 1% of the time, Pallas kernels for 0%

profile of v1, /device:TPU:30, one launch (start us, length us, event | category | flops | bytes accessed | tf_op | source)
XLA Modules:
  0.0 278.4 jit_solution(9452365454660945509)
XLA Ops:
  11.4 22.6 %all_gather.3 = bf16[768,512]{1,0:T(8,128)(2,1)S(1)} all-gather(bf16[24,512]{1,0:T(8,128)(2,1)} %param.15), channel_id=1, replica_groups=mesh['req'=32,'tp'=8] {'req'}, dimensions={0}, use_global_device_ids=true | all-gather | bytes 811008 | tf_op jit(solution)/shard_map/all_gather | solution.py:135
  34.6 50.0 %while.18 = (s32[]{:T(128)}, f32[64,1,4]{0,2,1:T(4,128)S(1)}, f32[64,1,4]{0,2,1:T(4,128)S(1)}, f32[64,1,4,128]{3,0,2,1:T(8,128)S(1)}, s32[2]{0:T(128)}, /*index=...) while((s32[]{:T(128)}, f32[64,1,4]{0,2,1:T(4,128)S(1)}, ...), condition=%wide.region_9.10_spmd.clone, body=%wide.region_6.9_spmd.clone.sunk | while | flops 136876160 | bytes 4351967 | solution.py:74
  37.4 1.4 fusion.85
  41.5 1.4 fusion.85
  43.9 1.4 fusion.82
  45.7 1.4 fusion.85
  49.9 1.4 fusion.85
  54.0 1.4 fusion.85
  58.2 1.4 fusion.85
  62.4 1.4 fusion.85
  66.5 1.4 fusion.85
  70.7 1.4 fusion.85
  74.8 1.4 fusion.85
  79.0 1.4 fusion.85
  83.2 1.4 fusion.85
  84.9 2.0 fusion.27
  89.2 120.3 %all-reduce = f32[768,4]{0,1:T(4,128)S(1)} all-reduce(f32[768,4]{0,1:T(4,128)S(1)} %fusion.26), channel_id=3, replica_groups=mesh['req'=32,'tp'=8] {'req'}, use_global_device_ids=true, to_apply=%region_11.12.clone | all-reduce | flops 3072 | bytes 24576
  212.0 2.9 %fusion.36 = f32[24,4096]{1,0:T(8,128)S(1)} fusion(bf16[512,4096]{1,0:T(8,128)(2,1)} %param.25, bf16[3,8,4,128]{3,2,1,0:T(4,128)(2,1)S(1)} %bitcast.93), kind=kOutput, calls=%fused_computation.56 | convolution fusion | flops 100663296 | bytes 4612096 | tf_op jit(solution)/shard_map/dot_general | solution.py:194
  214.9 1.9 collective-permute-start
  216.9 7.5 %collective-permute-done = f32[24,4096]{1,0:T(8,128)S(1)} collective-permute-done((f32[24,4096]{1,0:T(8,128)S(1)}, f32[24,4096]{1,0:T(8,128)S(1)}, u32[]{:S(2)}, u32[]{:S(2)}) %collective-permute-start) | collective-permute-done | bytes 393248 | tf_op jit(solution)/shard_map/ppermute | solution.py:18
  224.4 3.4 %collective-permute-start.1 = (f32[24,4096]{1,0:T(8,128)S(1)}, f32[24,4096]{1,0:T(8,128)S(1)}, u32[]{:S(2)}, u32[]{:S(2)}) collective-permute-start(f32[24,4096]{1,0:T(8,128)S(1)} %add.162), channel_id=1, source_target_pairs={{0,2},{1,3},{2,0},{3,1},{4,6},{5,7},{6,4},{7,5},{8,10},{9,11},{10,... | collective-permute-start | bytes 1179656 | tf_op jit(solution)/shard_map/ppermute | solution.py:18
  227.8 17.0 %collective-permute-done.1 = f32[24,4096]{1,0:T(8,128)S(1)} collective-permute-done((f32[24,4096]{1,0:T(8,128)S(1)}, f32[24,4096]{1,0:T(8,128)S(1)}, u32[]{:S(2)}, u32[]{:S(2)}) %collective-permute-start.1) | collective-permute-done | bytes 393248 | tf_op jit(solution)/shard_map/ppermute | solution.py:18
  244.8 7.8 %collective-permute-start.2 = (f32[24,4096]{1,0:T(8,128)S(1)}, f32[24,4096]{1,0:T(8,128)S(1)}, u32[]{:S(2)}, u32[]{:S(2)}) collective-permute-start(f32[24,4096]{1,0:T(8,128)S(1)} %add.163), channel_id=1, source_target_pairs={{0,4},{1,5},{2,6},{3,7},{4,0},{5,1},{6,2},{7,3},{8,12},{9,13},{10,... | collective-permute-start | bytes 1179656 | tf_op jit(solution)/shard_map/ppermute | solution.py:18
  252.6 17.9 %collective-permute-done.2 = f32[24,4096]{1,0:T(8,128)S(1)} collective-permute-done((f32[24,4096]{1,0:T(8,128)S(1)}, f32[24,4096]{1,0:T(8,128)S(1)}, u32[]{:S(2)}, u32[]{:S(2)}) %collective-permute-start.2) | collective-permute-done | bytes 393248 | tf_op jit(solution)/shard_map/ppermute | solution.py:18
  (206 shorter events, 41.0 us)
Async XLA Ops:
  7.2 202.7 %copy-start = (bf16[24,128,128]{2,1,0:T(8,128)(2,1)S(1)}, bf16[24,128,128]{2,1,0:T(8,128)(2,1)}, u32[]{:S(2)}) copy-start(bf16[24,128,128]{2,1,0:T(8,128)(2,1)} %param.20) | copy-start | bytes 2359300
  7.2 203.6 %reduce-scatter.3.cloned.1.call-start = ((), (), s32[]{:S(2)}) async-start(), calls=%async_computation.1 | async-start | bytes 1622016 | tf_op jit(solution)/shard_map/reduce_scatter | solution.py:147
  84.6 2.4 copy-start.2
  84.6 3.2 %copy-start.7 = (u32[256]{0:T(256)S(1)}, u32[256]{0:T(256)}, u32[]{:S(2)}) copy-start(u32[256]{0:T(256)} %constant.130) | copy-start | bytes 3076
  84.6 125.0 %copy-start.4 = (bf16[24,128]{1,0:T(8,128)(2,1)S(1)}, bf16[24,128]{1,0:T(8,128)(2,1)}, u32[]{:S(2)}) copy-start(bf16[24,128]{1,0:T(8,128)(2,1)} %param.17) | copy-start | bytes 18436
  84.6 125.1 %copy-start.6 = (bf16[24,128]{1,0:T(8,128)(2,1)S(1)}, bf16[24,128]{1,0:T(8,128)(2,1)}, u32[]{:S(2)}) copy-start(bf16[24,128]{1,0:T(8,128)(2,1)} %param.16) | copy-start | bytes 18436
  84.6 127.0 %copy-start.5 = (bf16[24,128,128]{2,1,0:T(8,128)(2,1)S(1)}, bf16[24,128,128]{2,1,0:T(8,128)(2,1)}, u32[]{:S(2)}) copy-start(bf16[24,128,128]{2,1,0:T(8,128)(2,1)} %param.21) | copy-start | bytes 2359300
  212.0 40.6 %copy-start.3 = (bf16[4096]{0:T(1024)(128)(2,1)S(1)}, bf16[4096]{0:T(1024)(128)(2,1)}, u32[]{:S(2)}) copy-start(bf16[4096]{0:T(1024)(128)(2,1)} %param.27) | copy-start | bytes 24580
  212.0 58.5 %copy-start.1 = (bf16[24,4096]{1,0:T(8,128)(2,1)S(1)}, bf16[24,4096]{1,0:T(8,128)(2,1)}, u32[]{:S(2)}) copy-start(bf16[24,4096]{1,0:T(8,128)(2,1)} %param.26) | copy-start | bytes 589828
  214.9 9.4 %collective-permute-start = (f32[24,4096]{1,0:T(8,128)S(1)}, f32[24,4096]{1,0:T(8,128)S(1)}, u32[]{:S(2)}, u32[]{:S(2)}) collective-permute-start(f32[24,4096]{1,0:T(8,128)S(1)} %fusion.36), channel_id=1, source_target_pairs={{0,1},{1,0},{2,3},{3,2},{4,5},{5,4},{6,7},{7,6},{8,9},{9,8},{10,11... | collective-permute-start | bytes 1179656 | tf_op jit(solution)/shard_map/ppermute | solution.py:18
  224.4 20.4 %collective-permute-start.1 = (f32[24,4096]{1,0:T(8,128)S(1)}, f32[24,4096]{1,0:T(8,128)S(1)}, u32[]{:S(2)}, u32[]{:S(2)}) collective-permute-start(f32[24,4096]{1,0:T(8,128)S(1)} %add.162), channel_id=1, source_target_pairs={{0,2},{1,3},{2,0},{3,1},{4,6},{5,7},{6,4},{7,5},{8,10},{9,11},{10,... | collective-permute-start | bytes 1179656 | tf_op jit(solution)/shard_map/ppermute | solution.py:18
  244.8 25.7 %collective-permute-start.2 = (f32[24,4096]{1,0:T(8,128)S(1)}, f32[24,4096]{1,0:T(8,128)S(1)}, u32[]{:S(2)}, u32[]{:S(2)}) collective-permute-start(f32[24,4096]{1,0:T(8,128)S(1)} %add.163), channel_id=1, source_target_pairs={{0,4},{1,5},{2,6},{3,7},{4,0},{5,1},{6,2},{7,3},{8,12},{9,13},{10,... | collective-permute-start | bytes 1179656 | tf_op jit(solution)/shard_map/ppermute | solution.py:18
Sparse Core Ops, SparseCore 0:
  87.1 86.9 reduce-scatter.2
